TPU v7x, 512 devices: a whole 4x8x8 slice. The times are simulated.
512 devices in a mesh: dp: 4 (over y_lo, core), seq: 4 (over x), fsdp: 32 (over y_hi, z).
Axes of the slice: x: 4, y: 8 (y_hi: 4, y_lo: 2; y = y_hi * 2 + y_lo), z: 8, core: 2. Of those that a mesh axis runs over, the one named last changes fastest.
Arguments:
- patches: bfloat16 [128, 768, 6144], P(('dp', 'fsdp'), 'seq'), may hold values from -100 to 100
- segments: int32 [128, 768], P(('dp', 'fsdp'), 'seq'), may hold values from 0 to 7, never falling along the last dimension, each value on 1 to 384 neighbouring positions
- qkv_weight: bfloat16 [6144, 384], P('fsdp'), may hold values from -0.078125 to 0.078125
- cotangent: bfloat16 [128, 768, 128], P(('dp', 'fsdp'), 'seq'), may hold values from -6 to 6
Outputs:
- input_grad: bfloat16 [128, 768, 6144], P(('dp', 'fsdp'), 'seq')
- weight_grad: float32 [6144, 384], P('fsdp')
Inputs may be any that keep to these rules, and one draw needn't show every extreme that they name: `segments`: within a sequence the image number never falls; each of the 8 images has 1 to 384 patches and one has exactly 384.
All inputs are finite; a program needn't handle non-finite values.
Results may differ from a plain program's by a relative error of at most 0.034.
The roundings to bfloat16 on the way count: a program that leaves them out, or rounds other values in their place, can miss the bound.
Values may be sent and summed in bfloat16 or wider, within the bound.
No kernel may reach another device: no remote copies, remote signals or barrier semaphores. Data moves between devices by JAX's collectives and lax.ppermute only.
A program may use at most 64 MiB of HBM per device.

v0:
```python
import functools
import jax
import jax.numpy as jnp
from jax import lax
from jax.sharding import PartitionSpec as P


def contract_first(left, right):
    return lax.dot_general(
        left, right, (((0,), (0,)), ((), ())), preferred_element_type=jnp.float32
    )


def contract_last(left, right):
    return lax.dot_general(
        left, right, (((1,), (1,)), ((), ())), preferred_element_type=jnp.float32
    )


def dp_partner(x, bit):
    pairs = [(i, i ^ bit) for i in range(lax.axis_size("dp"))]
    return lax.ppermute(x, "dp", perm=pairs)


class Ring:

    def __init__(self, axis, size, inner):
        self.axis, self.size, self.inner = (axis, size, inner)

    def total(self):
        return lax.axis_size(self.axis)

    def position(self):
        return lax.axis_index(self.axis) // self.inner % self.size

    def shift(self, x, step):
        n, inner, total = (self.size, self.inner, self.total())
        pairs = []
        for i in range(total):
            pos = i // inner % n
            base = i - pos * inner
            pairs.append((i, base + (pos + step) % n * inner))
        return lax.ppermute(x, self.axis, perm=pairs)


def ring_gather(x, ring, beside=None, late=None):
    n = ring.size
    got, slot = ([x], {0: 0})
    cw, ccw = (x, x)
    last_cw = n - 1 if (n - 1) % 2 == 1 else n - 2
    last_ccw = n - 1 if (n - 1) % 2 == 0 else n - 2
    for t in range(1, n):
        if t % 2 == 1:
            cw = ring.shift(cw, 1)
            if t == 1 and beside is not None:
                cw, beside = lax.optimization_barrier((cw, beside))
            if t == last_cw and late is not None:
                cw, late = lax.optimization_barrier((cw, late))
            slot[(n - (t + 1) // 2) % n] = len(got)
            got.append(cw)
        else:
            ccw = ring.shift(ccw, -1)
            if t == last_ccw and late is not None:
                value, make = late
                ccw, value = lax.optimization_barrier((ccw, value))
                late = make(value)
            slot[t // 2] = len(got)
            got.append(ccw)
    if late is not None:
        return (jnp.stack(got), [slot[k] for k in range(n)], late)
    return (jnp.stack(got), [slot[k] for k in range(n)], beside)


def ring_reduce_scatter(blocks, ring, axis=0, beside=None):
    n = ring.size
    me = ring.position()

    def pick(index):
        return lax.dynamic_index_in_dim(blocks, index % n, axis=axis, keepdims=False)

    total = pick(me)
    if n == 1:
        return (total, beside)
    up, down = (n // 2, (n - 1) // 2)
    acc = pick(me + up)
    for t in range(1, up + 1):
        acc = ring.shift(acc.astype(jnp.bfloat16), 1)
        if t == 1 and beside is not None:
            acc, beside = lax.optimization_barrier((acc, beside))
        acc = acc.astype(jnp.float32)
        if t < up:
            acc = acc + pick(me + up - t)
    total = total + acc
    if down:
        acc = pick(me - down)
        for t in range(1, down + 1):
            acc = ring.shift(acc.astype(jnp.bfloat16), -1).astype(jnp.float32)
            if t < down:
                acc = acc + pick(me - down + t)
        total = total + acc
    return (total, beside)


def shards(patches, segments, qkv_weight, cotangent, inner_fsdp):
    features = patches[0]
    image_ids = segments[0]
    grad_out = cotangent[0]
    width_head = cotangent.shape[2]
    width_all = qkv_weight.shape[1]
    rows_w = qkv_weight.shape[0]
    half = width_all // 2
    scale = width_head ** (-0.5)
    core = lax.axis_index("dp") % 2
    first = core == 0
    outer_fsdp = lax.axis_size("fh")
    n_fsdp = outer_fsdp * inner_fsdp
    ring_y = Ring("fh", outer_fsdp, 1)
    ring_z = Ring("fz", inner_fsdp, 1)
    ring_x = Ring("seq", lax.axis_size("seq"), 1)
    w_mine = lax.dynamic_slice_in_dim(qkv_weight, core * half, half, axis=1)
    stack_y = lax.all_gather(w_mine, "fh", axis=0, tiled=False)
    relayout = lambda f: f.reshape(f.shape[0], outer_fsdp, inner_fsdp, rows_w)
    stack_zy, slot_z, blocked = ring_gather(stack_y, ring_z, late=(features, relayout))
    flat = stack_zy.reshape(-1, rows_w, half)
    me_y, me_z = (ring_y.position(), ring_z.position())
    absolute = jnp.arange(n_fsdp, dtype=jnp.int32)
    rel_z = (absolute % inner_fsdp - me_z) % inner_fsdp
    order = jnp.asarray(slot_z, jnp.int32)[rel_z] * outer_fsdp + absolute // inner_fsdp
    w_mine_all = jnp.take(flat, order, axis=0, mode="clip").reshape(n_fsdp * rows_w, half)
    w_other_all = dp_partner(w_mine_all, 1)
    h_mine = jnp.dot(features, w_mine_all, preferred_element_type=jnp.float32)
    h_other = jnp.dot(features, w_other_all, preferred_element_type=jnp.float32)
    projected = jnp.where(
        first,
        jnp.concatenate([h_mine, h_other], axis=1),
        jnp.concatenate([h_other, h_mine], axis=1),
    )
    heads = projected.astype(jnp.bfloat16)
    n_rows = features.shape[0]
    n_x = ring_x.size
    me_x = ring_x.position()
    ids_col = jnp.broadcast_to(image_ids.astype(jnp.bfloat16)[:, None], (n_rows, width_head))
    packed = jnp.concatenate([heads, grad_out, ids_col], axis=1)
    packed_all = lax.all_gather(packed, "seq", axis=0, tiled=True)
    query_all = packed_all[:, :width_head]
    keys_all = packed_all[:, width_head : 2 * width_head]
    values_all = packed_all[:, 2 * width_head : 3 * width_head]
    grad_out_all = packed_all[:, 3 * width_head : 4 * width_head]
    images_all = packed_all[:, 4 * width_head]
    scores = contract_last(query_all, keys_all) * scale
    allowed = images_all[:, None] == images_all[None, :]
    highest = jnp.max(jnp.where(allowed, scores, -jnp.inf), axis=1)
    summed = jnp.sum(jnp.where(allowed, jnp.exp(scores - highest[:, None]), 0.0), axis=1)
    log_total = highest + jnp.log(summed)
    attention = jnp.where(allowed, jnp.exp(scores - log_total[:, None]), 0.0)
    attention_low = attention.astype(jnp.bfloat16)
    output = jnp.dot(attention_low, values_all, preferred_element_type=jnp.float32)
    delta_rows = jnp.sum(grad_out_all.astype(jnp.float32) * output, axis=1)
    grad_attention = contract_last(grad_out_all, values_all)
    grad_scores = (attention * (grad_attention - delta_rows[:, None]) * scale).astype(jnp.bfloat16)
    start = me_x * n_rows
    own_rows = lax.dynamic_slice_in_dim(grad_scores, start, n_rows, axis=0)
    own_cols = lax.dynamic_slice_in_dim(grad_scores, start, n_rows, axis=1)
    own_attention = lax.dynamic_slice_in_dim(attention_low, start, n_rows, axis=1)
    grad_query = jnp.dot(own_rows, keys_all, preferred_element_type=jnp.float32)
    grad_key = contract_first(own_cols, query_all)
    grad_value = contract_first(own_attention, grad_out_all)
    grad_heads = jnp.concatenate([grad_query, grad_key, grad_value], axis=1).astype(jnp.bfloat16)
    g_lo = grad_heads[:, :half]
    g_hi = grad_heads[:, half:]
    g_mine = jnp.where(first, g_lo, g_hi)
    g_other = jnp.where(first, g_hi, g_lo)
    input_grad = (contract_last(g_mine, w_mine_all) + contract_last(g_other, w_other_all)).astype(
        jnp.bfloat16
    )
    wg_other = jnp.einsum("pyzd,pc->zydc", blocked, g_other, preferred_element_type=jnp.float32)
    wg_from_partner = dp_partner(wg_other.astype(jnp.bfloat16), 1)
    wg_mine = jnp.einsum("pyzd,pc->zydc", blocked, g_mine, preferred_element_type=jnp.float32)
    wg_mine, wg_from_partner = lax.optimization_barrier((wg_mine, wg_from_partner))
    blocks = wg_mine + wg_from_partner.astype(jnp.float32)
    over_z, input_grad = ring_reduce_scatter(blocks, ring_z, axis=0, beside=input_grad)
    over_fsdp, _ = ring_reduce_scatter(over_z, ring_y)
    by_seq = lax.all_gather(over_fsdp, "seq", axis=0, tiled=False)
    over_seq = by_seq[0]
    for s_i in range(1, by_seq.shape[0]):
        over_seq = over_seq + by_seq[s_i]
    by_dp = lax.all_gather(over_seq, "dp", axis=0, tiled=False)
    halves = []
    for c in range(2):
        part = by_dp[c]
        for d in range(c + 2, by_dp.shape[0], 2):
            part = part + by_dp[d]
        halves.append(part)
    weight_grad = jnp.concatenate(halves, axis=1)
    return (input_grad[None], weight_grad)


def inner_ring_size(mesh):
    axis = mesh.axis_names.index("fsdp")
    line = mesh.devices[tuple((0 if a != axis else slice(None) for a in range(mesh.devices.ndim)))]
    line = list(line)
    if not hasattr(line[0], "coords"):
        return len(line)
    count = 1
    while count < len(line) and line[count].coords[1] == line[0].coords[1]:
        count += 1
    return count


def solution(mesh):
    inner = inner_ring_size(mesh)
    sizes = dict(zip(mesh.axis_names, mesh.devices.shape))
    split = jax.sharding.Mesh(
        mesh.devices.reshape(sizes["dp"], sizes["seq"], sizes["fsdp"] // inner, inner),
        ("dp", "seq", "fh", "fz"),
    )
    rows = ("dp", "fh", "fz")
    placed = (P(rows, "seq", None), P(rows, "seq"), P(("fh", "fz"), None), P(rows, "seq", None))
    return jax.shard_map(
        functools.partial(shards, inner_fsdp=inner),
        mesh=split,
        in_specs=placed,
        out_specs=(P(rows, "seq", None), P(("fh", "fz"), None)),
        check_vma=False,
    )
```

profile of v0, /device:TPU:75, one launch (start us, length us, event | category | flops | bytes accessed | tf_op | source)
XLA Modules:
  0.0 222.7 jit_solution(9267431359710863556)
XLA Ops:
  1.6 13.7 %all-gather = bf16[768,192]{1,0:T(8,128)(2,1)S(1)} all-gather(bf16[192,192]{1,0:T(8,128)(2,1)S(1)} %constant_dynamic-slice_fusion), channel_id=2, replica_groups=mesh['dp'=4,'seq'=4,'fh'=4,'fz'=8] {'fh'}, dimensions={0}, use_global_device_ids=true | all-gather | bytes 368640 | tf_op jit(solution)/shard_map/all_gather | solution.py:121
  15.3 4.0 %collective-permute-start = (bf16[4,192,192]{2,1,0:T(8,128)(2,1)S(1)}, bf16[4,192,192]{2,1,0:T(8,128)(2,1)}, u32[]{:S(2)}, u32[]{:S(2)}) collective-permute-start(bf16[4,192,192]{2,1,0:T(8,128)(2,1)S(1)} %bitcast.108), channel_id=1, source_target_pairs={{0,1},{1,2},{2,3},{3,4},{4,5},{5,6},{6,7},{7,0},{8,9},{9,10},{10,1... | collective-permute-start | bytes 884744 | tf_op jit(solution)/shard_map/ppermute | solution.py:43
  24.0 4.0 %collective-permute-start.2 = (bf16[4,192,192]{2,1,0:T(8,128)(2,1)}, bf16[4,192,192]{2,1,0:T(8,128)(2,1)S(1)}, u32[]{:S(2)}, u32[]{:S(2)}) collective-permute-start(bf16[4,192,192]{2,1,0:T(8,128)(2,1)} %collective-permute-done), channel_id=1, source_target_pairs={{0,1},{1,2},{2,3},{3,4},{4,5},{5,6},{6,7},{7,0},{8,9},{9,10},{10,1... | collective-permute-start | bytes 884744 | tf_op jit(solution)/shard_map/ppermute | solution.py:43
  29.8 6.4 %collective-permute-start.3 = (bf16[4,192,192]{2,1,0:T(8,128)(2,1)S(1)}, bf16[4,192,192]{2,1,0:T(8,128)(2,1)S(1)}, u32[]{:S(2)}, u32[]{:S(2)}) collective-permute-start(bf16[4,192,192]{2,1,0:T(8,128)(2,1)S(1)} %collective-permute-done.1), channel_id=1, source_target_pairs={{0,7},{1,0},{2,1},{3,2},{4,3},{5,4},{6,5},{7,6},{8,15},{9,8},{10,9... | collective-permute-start | bytes 884744 | tf_op jit(solution)/shard_map/ppermute | solution.py:43
  40.9 4.6 %collective-permute-start.5 = (bf16[4,192,192]{2,1,0:T(8,128)(2,1)S(1)}, bf16[4,192,192]{2,1,0:T(8,128)(2,1)S(1)}, u32[]{:S(2)}, u32[]{:S(2)}) collective-permute-start(bf16[4,192,192]{2,1,0:T(8,128)(2,1)S(1)} %collective-permute-done.3), channel_id=1, source_target_pairs={{0,7},{1,0},{2,1},{3,2},{4,3},{5,4},{6,5},{7,6},{8,15},{9,8},{10,9... | collective-permute-start | bytes 884744 | tf_op jit(solution)/shard_map/ppermute | solution.py:43
  51.5 4.5 %reshape.141 = bf16[192,4,8,192]{3,2,1,0:T(8,128)(2,1)} reshape(bf16[192,6144]{1,0:T(8,128)(2,1)S(1)} %bitcast.105) | data formatting | bytes 4718592 | tf_op jit(solution)/shard_map/reshape | solution.py:122
  60.0 2.6 %gather_fusion.1 = bf16[32,192,192]{2,1,0:T(8,128)(2,1)S(1)} fusion(bf16[32,192,192]{2,1,0:T(8,128)(2,1)} %bitcast.106, s32[1024]{0:T(1024)S(1)} %pad_clamp_fusion), kind=kCustom, calls=%fused_computation.1 | custom fusion | bytes 4718720 | tf_op jit(solution)/shard_map/jit(_take)/gather | solution.py:129
  62.6 2.6 %copy.31 = bf16[6144,192]{0,1:T(8,128)(2,1)} copy(bf16[6144,192]{1,0:T(8,128)(2,1)S(1)} %bitcast.102) | data formatting | bytes 4718592 | tf_op jit(solution)/shard_map/reshape | solution.py:129
  65.2 10.2 %collective-permute-start.7 = (bf16[6144,192]{0,1:T(8,128)(2,1)}, bf16[6144,192]{0,1:T(8,128)(2,1)}, u32[]{:S(2)}, u32[]{:S(2)}) collective-permute-start(bf16[6144,192]{0,1:T(8,128)(2,1)} %copy.31), channel_id=1, source_target_pairs={{0,128},{128,0},{256,384},{384,256},{1,129},{129,1},{257,385},{385... | collective-permute-start | bytes 7077896 | tf_op jit(solution)/shard_map/ppermute | solution.py:22
  75.5 2.6 %convolution_bitcast_fusion.1 = bf16[192,192]{1,0:T(8,128)(2,1)S(1)} fusion(bf16[6144,192]{1,0:T(8,128)(2,1)S(1)} %bitcast.103, bf16[1,192,6144]{2,1,0:T(8,128)(2,1)} %param.5), kind=kOutput, calls=%fused_computation.21 | convolution fusion | flops 452984832 | bytes 4792320 | tf_op jit(solution)/shard_map/dot_general | solution.py:131
  79.9 2.5 %convolution_bitcast_fusion = bf16[192,192]{1,0:T(8,128)(2,1)S(1)} fusion(bf16[6144,192]{0,1:T(8,128)(2,1)} %collective-permute-done.7, bf16[1,192,6144]{2,1,0:T(8,128)(2,1)S(1)} %copy-done.5), kind=kOutput, calls=%fused_computation.20 | convolution fusion | flops 452984832 | bytes 4792320 | tf_op jit(solution)/shard_map/dot_general | solution.py:132
  82.7 12.4 %all_gather.21 = bf16[768,640]{1,0:T(8,128)(2,1)S(1)} all-gather(bf16[192,640]{1,0:T(8,128)(2,1)S(1)} %pad_maximum_fusion.1), channel_id=1, replica_groups=mesh['dp'=4,'seq'=4,'fh'=4,'fz'=8] {'seq'}, dimensions={0}, use_global_device_ids=true | all-gather | bytes 1228800 | tf_op jit(solution)/shard_map/all_gather | solution.py:144
  99.5 4.1 %convert_bitcast_fusion = bf16[8,4,192,192]{2,3,0,1:T(8,128)(2,1)} fusion(bf16[192,4,8,192]{3,2,1,0:T(8,128)(2,1)S(1)} %copy-done.1, pred[]{:T(512)S(6)} %eq.39, bf16[192,128]{1,0:T(8,128)(2,1)S(1)} %convolution_convert_fusion.1, bf16[192,128]{1,0:T(8,128)(2,1)S(1)} %convolution_convert_fusion.2, bf16[192,128]{1,0:T(8,128)(2,1)S(1)} %convolution_convert_fusion), kind=kOutput, calls=%fused_computation.8 | convolution fusion | flops 454496256 | bytes 4866049 | tf_op jit(solution)/shard_map/pyzd,pc->zydc/dot_general | solution.py:176
  103.6 5.4 %collective-permute-start.8 = (bf16[8,4,192,192]{2,3,0,1:T(8,128)(2,1)}, bf16[8,4,192,192]{2,3,0,1:T(8,128)(2,1)}, u32[]{:S(2)}, u32[]{:S(2)}) collective-permute-start(bf16[8,4,192,192]{2,3,0,1:T(8,128)(2,1)} %convert_bitcast_fusion), channel_id=1, source_target_pairs={{0,128},{128,0},{256,384},{384,256},{1,129},{129,1},{257,385},{385... | collective-permute-start | bytes 7077896 | tf_op jit(solution)/shard_map/ppermute | solution.py:22
  111.0 2.4 %fusion.5 = f32[8,4,192,192]{2,3,0,1:T(8,128)S(1)} fusion(bf16[192,4,8,192]{3,2,1,0:T(8,128)(2,1)S(1)} %copy-done.2, pred[]{:T(512)S(6)} %eq.39, bf16[192,128]{1,0:T(8,128)(2,1)S(1)} %convolution_convert_fusion.1, bf16[192,128]{1,0:T(8,128)(2,1)S(1)} %convolution_convert_fusion.2, bf16[192,128]{1,0:T(8,128)(2,1)S(1)} %convolution_convert_fusion), kind=kOutput, calls=%fused_computation.13 | convolution fusion | flops 453316608 | bytes 7225345 | tf_op jit(solution)/shard_map/pyzd,pc->zydc/dot_general | solution.py:178
  114.5 3.0 %convert_add_fusion = f32[8,4,192,192]{2,3,0,1:T(8,128)S(1)} fusion(f32[8,4,192,192]{2,3,0,1:T(8,128)S(1)} %fusion.5, bf16[8,4,192,192]{2,3,0,1:T(8,128)(2,1)} %collective-permute-done.8), kind=kLoop, calls=%fused_computation.4 | loop fusion | flops 2359296 | bytes 11796480 | tf_op jit(solution)/shard_map/add | solution.py:180
  117.6 2.1 collective-permute-start.9
  119.7 3.9 %fusion = bf16[192,6144]{1,0:T(8,128)(2,1)} fusion(f32[192,6144]{1,0:T(8,128)S(1)} %fusion.54, bf16[6144,192]{0,1:T(8,128)(2,1)} %collective-permute-done.7, pred[]{:T(512)S(6)} %eq.39, bf16[192,128]{1,0:T(8,128)(2,1)S(1)} %convolution_convert_fusion.1, bf16[192,128]{1,0:T(8,128)(2,1)S(1)} %convolution_convert_fusion.2, ...), kind=kOutput, calls=%fused_computation.3 | convolution fusion | flops 455675904 | bytes 9584641 | tf_op jit(solution)/shard_map/dot_general | solution.py:15
  123.6 4.7 %collective-permute-start.13 = (bf16[4,192,192]{1,2,0:T(8,128)(2,1)S(1)}, bf16[4,192,192]{1,2,0:T(8,128)(2,1)S(1)}, u32[]{:S(2)}, u32[]{:S(2)}) collective-permute-start(bf16[4,192,192]{1,2,0:T(8,128)(2,1)S(1)} %get-tuple-element.26), channel_id=1, source_target_pairs={{0,7},{1,0},{2,1},{3,2},{4,3},{5,4},{6,5},{7,6},{8,15},{9,8},{10,9... | collective-permute-start | bytes 884744 | tf_op jit(solution)/shard_map/ppermute | solution.py:43
  128.4 3.3 %collective-permute-done.9 = bf16[4,192,192]{1,2,0:T(8,128)(2,1)S(1)} collective-permute-done((bf16[4,192,192]{1,2,0:T(8,128)(2,1)S(1)}, bf16[4,192,192]{1,2,0:T(8,128)(2,1)S(1)}, u32[]{:S(2)}, u32[]{:S(2)}) %collective-permute-start.9) | collective-permute-done | bytes 294944 | tf_op jit(solution)/shard_map/ppermute | solution.py:43
  133.7 4.2 %collective-permute-done.13 = bf16[4,192,192]{1,2,0:T(8,128)(2,1)S(1)} collective-permute-done((bf16[4,192,192]{1,2,0:T(8,128)(2,1)S(1)}, bf16[4,192,192]{1,2,0:T(8,128)(2,1)S(1)}, u32[]{:S(2)}, u32[]{:S(2)}) %collective-permute-start.13) | collective-permute-done | bytes 294944 | tf_op jit(solution)/shard_map/ppermute | solution.py:43
  137.9 6.4 %collective-permute-done.10 = bf16[4,192,192]{1,2,0:T(8,128)(2,1)S(1)} collective-permute-done((bf16[4,192,192]{1,2,0:T(8,128)(2,1)S(1)}, bf16[4,192,192]{1,2,0:T(8,128)(2,1)S(1)}, u32[]{:S(2)}, u32[]{:S(2)}) %collective-permute-start.10) | collective-permute-done | bytes 294944 | tf_op jit(solution)/shard_map/ppermute | solution.py:43
  147.7 4.3 %collective-permute-start.14 = (bf16[4,192,192]{1,2,0:T(8,128)(2,1)S(1)}, bf16[4,192,192]{1,2,0:T(8,128)(2,1)S(1)}, u32[]{:S(2)}, u32[]{:S(2)}) collective-permute-start(bf16[4,192,192]{1,2,0:T(8,128)(2,1)S(1)} %get-tuple-element.25), channel_id=1, source_target_pairs={{0,7},{1,0},{2,1},{3,2},{4,3},{5,4},{6,5},{7,6},{8,15},{9,8},{10,9... | collective-permute-start | bytes 884744 | tf_op jit(solution)/shard_map/ppermute | solution.py:43
  152.1 5.3 %collective-permute-done.11 = bf16[4,192,192]{1,2,0:T(8,128)(2,1)S(1)} collective-permute-done((bf16[4,192,192]{1,2,0:T(8,128)(2,1)S(1)}, bf16[4,192,192]{1,2,0:T(8,128)(2,1)S(1)}, u32[]{:S(2)}, u32[]{:S(2)}) %collective-permute-start.11) | collective-permute-done | bytes 294944 | tf_op jit(solution)/shard_map/ppermute | solution.py:43
  159.8 5.2 %collective-permute-start.12 = (bf16[4,192,192]{1,2,0:T(8,128)(2,1)S(1)}, bf16[4,192,192]{1,2,0:T(8,128)(2,1)S(1)}, u32[]{:S(2)}, u32[]{:S(2)}) collective-permute-start(bf16[4,192,192]{1,2,0:T(8,128)(2,1)S(1)} %get-tuple-element.22), channel_id=1, source_target_pairs={{0,1},{1,2},{2,3},{3,4},{4,5},{5,6},{6,7},{7,0},{8,9},{9,10},{10,1... | collective-permute-start | bytes 884744 | tf_op jit(solution)/shard_map/ppermute | solution.py:43
  167.1 3.3 %collective-permute-done.12 = bf16[4,192,192]{1,2,0:T(8,128)(2,1)S(1)} collective-permute-done((bf16[4,192,192]{1,2,0:T(8,128)(2,1)S(1)}, bf16[4,192,192]{1,2,0:T(8,128)(2,1)S(1)}, u32[]{:S(2)}, u32[]{:S(2)}) %collective-permute-start.12) | collective-permute-done | bytes 294944 | tf_op jit(solution)/shard_map/ppermute | solution.py:43
  170.4 4.8 %collective-permute-done.15 = bf16[4,192,192]{1,2,0:T(8,128)(2,1)S(1)} collective-permute-done((bf16[4,192,192]{1,2,0:T(8,128)(2,1)S(1)}, bf16[4,192,192]{1,2,0:T(8,128)(2,1)S(1)}, u32[]{:S(2)}, u32[]{:S(2)}) %collective-permute-start.15) | collective-permute-done | bytes 294944 | tf_op jit(solution)/shard_map/ppermute | solution.py:43
  176.5 2.7 %collective-permute-start.16 = (bf16[192,192]{0,1:T(8,128)(2,1)S(1)}, bf16[192,192]{0,1:T(8,128)(2,1)S(1)}, u32[]{:S(2)}, u32[]{:S(2)}) collective-permute-start(bf16[192,192]{0,1:T(8,128)(2,1)S(1)} %get-tuple-element.30), channel_id=1, source_target_pairs={{0,8},{8,16},{16,24},{24,0},{1,9},{9,17},{17,25},{25,1},{2,10},{10... | collective-permute-start | bytes 221192 | tf_op jit(solution)/shard_map/ppermute | solution.py:43
  179.3 4.7 %collective-permute-start.18 = (bf16[192,192]{0,1:T(8,128)(2,1)S(1)}, bf16[192,192]{0,1:T(8,128)(2,1)S(1)}, u32[]{:S(2)}, u32[]{:S(2)}) collective-permute-start(bf16[192,192]{0,1:T(8,128)(2,1)S(1)} %get-tuple-element.31), channel_id=1, source_target_pairs={{0,24},{8,0},{16,8},{24,16},{1,25},{9,1},{17,9},{25,17},{2,26},{10... | collective-permute-start | bytes 221192 | tf_op jit(solution)/shard_map/ppermute | solution.py:43
  186.5 5.4 %collective-permute-done.17 = bf16[192,192]{0,1:T(8,128)(2,1)S(1)} collective-permute-done((bf16[192,192]{0,1:T(8,128)(2,1)S(1)}, bf16[192,192]{0,1:T(8,128)(2,1)S(1)}, u32[]{:S(2)}, u32[]{:S(2)}) %collective-permute-start.17) | collective-permute-done | bytes 73760 | tf_op jit(solution)/shard_map/ppermute | solution.py:43
  192.1 11.0 %all-gather.1 = f32[768,192]{1,0:T(8,128)S(1)} all-gather(f32[192,192]{1,0:T(8,128)S(1)} %copy.39), channel_id=3, replica_groups=mesh['dp'=4,'seq'=4,'fh'=4,'fz'=8] {'seq'}, dimensions={0}, use_global_device_ids=true | all-gather | bytes 737280 | tf_op jit(solution)/shard_map/all_gather | solution.py:183
  203.1 18.7 %all_gather.24 = f32[4,192,192]{2,1,0:T(8,128)S(1)} all-gather(f32[1,192,192]{2,1,0:T(8,128)S(1)} %fusion.28), channel_id=1, replica_groups=mesh['dp'=4,'seq'=4,'fh'=4,'fz'=8] {'dp'}, dimensions={0}, use_global_device_ids=true | all-gather | bytes 737280 | tf_op jit(solution)/shard_map/all_gather | solution.py:187
  (76 shorter events, 46.4 us)
Async XLA Ops:
  0.6 0.9 copy-start
  15.3 8.7 %collective-permute-start = (bf16[4,192,192]{2,1,0:T(8,128)(2,1)S(1)}, bf16[4,192,192]{2,1,0:T(8,128)(2,1)}, u32[]{:S(2)}, u32[]{:S(2)}) collective-permute-start(bf16[4,192,192]{2,1,0:T(8,128)(2,1)S(1)} %bitcast.108), channel_id=1, source_target_pairs={{0,1},{1,2},{2,3},{3,4},{4,5},{5,6},{6,7},{7,0},{8,9},{9,10},{10,1... | collective-permute-start | bytes 884744 | tf_op jit(solution)/shard_map/ppermute | solution.py:43
  19.3 10.5 %collective-permute-start.1 = (bf16[4,192,192]{2,1,0:T(8,128)(2,1)S(1)}, bf16[4,192,192]{2,1,0:T(8,128)(2,1)S(1)}, u32[]{:S(2)}, u32[]{:S(2)}) collective-permute-start(bf16[4,192,192]{2,1,0:T(8,128)(2,1)S(1)} %bitcast.109), channel_id=1, source_target_pairs={{0,7},{1,0},{2,1},{3,2},{4,3},{5,4},{6,5},{7,6},{8,15},{9,8},{10,9... | collective-permute-start | bytes 884744 | tf_op jit(solution)/shard_map/ppermute | solution.py:43
  22.1 29.4 %copy-start.4 = (bf16[1,192,6144]{2,1,0:T(8,128)(2,1)S(1)}, bf16[1,192,6144]{2,1,0:T(8,128)(2,1)}, u32[]{:S(2)}) copy-start(bf16[1,192,6144]{2,1,0:T(8,128)(2,1)} %param.5) | copy-start | bytes 7077892
  24.0 13.9 %collective-permute-start.2 = (bf16[4,192,192]{2,1,0:T(8,128)(2,1)}, bf16[4,192,192]{2,1,0:T(8,128)(2,1)S(1)}, u32[]{:S(2)}, u32[]{:S(2)}) collective-permute-start(bf16[4,192,192]{2,1,0:T(8,128)(2,1)} %collective-permute-done), channel_id=1, source_target_pairs={{0,1},{1,2},{2,3},{3,4},{4,5},{5,6},{6,7},{7,0},{8,9},{9,10},{10,1... | collective-permute-start | bytes 884744 | tf_op jit(solution)/shard_map/ppermute | solution.py:43
  29.8 11.1 %collective-permute-start.3 = (bf16[4,192,192]{2,1,0:T(8,128)(2,1)S(1)}, bf16[4,192,192]{2,1,0:T(8,128)(2,1)S(1)}, u32[]{:S(2)}, u32[]{:S(2)}) collective-permute-start(bf16[4,192,192]{2,1,0:T(8,128)(2,1)S(1)} %collective-permute-done.1), channel_id=1, source_target_pairs={{0,7},{1,0},{2,1},{3,2},{4,3},{5,4},{6,5},{7,6},{8,15},{9,8},{10,9... | collective-permute-start | bytes 884744 | tf_op jit(solution)/shard_map/ppermute | solution.py:43
  37.9 9.8 %collective-permute-start.4 = (bf16[4,192,192]{2,1,0:T(8,128)(2,1)S(1)}, bf16[4,192,192]{2,1,0:T(8,128)(2,1)}, u32[]{:S(2)}, u32[]{:S(2)}) collective-permute-start(bf16[4,192,192]{2,1,0:T(8,128)(2,1)S(1)} %collective-permute-done.2), channel_id=1, source_target_pairs={{0,1},{1,2},{2,3},{3,4},{4,5},{5,6},{6,7},{7,0},{8,9},{9,10},{10,1... | collective-permute-start | bytes 884744 | tf_op jit(solution)/shard_map/ppermute | solution.py:43
  40.9 10.5 %collective-permute-start.5 = (bf16[4,192,192]{2,1,0:T(8,128)(2,1)S(1)}, bf16[4,192,192]{2,1,0:T(8,128)(2,1)S(1)}, u32[]{:S(2)}, u32[]{:S(2)}) collective-permute-start(bf16[4,192,192]{2,1,0:T(8,128)(2,1)S(1)} %collective-permute-done.3), channel_id=1, source_target_pairs={{0,7},{1,0},{2,1},{3,2},{4,3},{5,4},{6,5},{7,6},{8,15},{9,8},{10,9... | collective-permute-start | bytes 884744 | tf_op jit(solution)/shard_map/ppermute | solution.py:43
  47.7 10.5 %collective-permute-start.6 = (bf16[4,192,192]{2,1,0:T(8,128)(2,1)}, bf16[4,192,192]{2,1,0:T(8,128)(2,1)}, u32[]{:S(2)}, u32[]{:S(2)}) collective-permute-start(bf16[4,192,192]{2,1,0:T(8,128)(2,1)} %collective-permute-done.4), channel_id=1, source_target_pairs={{0,1},{1,2},{2,3},{3,4},{4,5},{5,6},{6,7},{7,0},{8,9},{9,10},{10,1... | collective-permute-start | bytes 884744 | tf_op jit(solution)/shard_map/ppermute | solution.py:43
  62.6 12.8 %copy-start.7 = (s32[1,192]{1,0:T(1,128)S(1)}, s32[1,192]{1,0:T(1,128)}, u32[]{:S(2)}) copy-start(s32[1,192]{1,0:T(1,128)} %param.6) | copy-start | bytes 2308
  65.2 14.7 %collective-permute-start.7 = (bf16[6144,192]{0,1:T(8,128)(2,1)}, bf16[6144,192]{0,1:T(8,128)(2,1)}, u32[]{:S(2)}, u32[]{:S(2)}) collective-permute-start(bf16[6144,192]{0,1:T(8,128)(2,1)} %copy.31), channel_id=1, source_target_pairs={{0,128},{128,0},{256,384},{384,256},{1,129},{129,1},{257,385},{385... | collective-permute-start | bytes 7077896 | tf_op jit(solution)/shard_map/ppermute | solution.py:22
  75.5 4.4 %copy-start.5 = (bf16[1,192,6144]{2,1,0:T(8,128)(2,1)S(1)}, bf16[1,192,6144]{2,1,0:T(8,128)(2,1)}, u32[]{:S(2)}) copy-start(bf16[1,192,6144]{2,1,0:T(8,128)(2,1)} %param.5) | copy-start | bytes 7077892
  78.1 4.5 %copy-start.6 = (bf16[1,192,128]{2,1,0:T(8,128)(2,1)S(1)}, bf16[1,192,128]{2,1,0:T(8,128)(2,1)}, u32[]{:S(2)}) copy-start(bf16[1,192,128]{2,1,0:T(8,128)(2,1)} %param.8) | copy-start | bytes 147460
  97.6 1.9 copy-start.1
  103.6 10.9 %collective-permute-start.8 = (bf16[8,4,192,192]{2,3,0,1:T(8,128)(2,1)}, bf16[8,4,192,192]{2,3,0,1:T(8,128)(2,1)}, u32[]{:S(2)}, u32[]{:S(2)}) collective-permute-start(bf16[8,4,192,192]{2,3,0,1:T(8,128)(2,1)} %convert_bitcast_fusion), channel_id=1, source_target_pairs={{0,128},{128,0},{256,384},{384,256},{1,129},{129,1},{257,385},{385... | collective-permute-start | bytes 7077896 | tf_op jit(solution)/shard_map/ppermute | solution.py:22
  109.1 1.9 copy-start.2
  117.5 14.1 %copy-start.3 = (f32[8,4,192,192]{2,3,0,1:T(8,128)}, f32[8,4,192,192]{2,3,0,1:T(8,128)S(1)}, u32[]{:S(2)}) copy-start(f32[8,4,192,192]{2,3,0,1:T(8,128)S(1)} %convert_add_fusion) | copy-start | bytes 14155780
  117.6 14.0 %collective-permute-start.9 = (bf16[4,192,192]{1,2,0:T(8,128)(2,1)S(1)}, bf16[4,192,192]{1,2,0:T(8,128)(2,1)S(1)}, u32[]{:S(2)}, u32[]{:S(2)}) collective-permute-start(bf16[4,192,192]{1,2,0:T(8,128)(2,1)S(1)} %get-tuple-element.27), channel_id=1, source_target_pairs={{0,1},{1,2},{2,3},{3,4},{4,5},{5,6},{6,7},{7,0},{8,9},{9,10},{10,1... | collective-permute-start | bytes 884744 | tf_op jit(solution)/shard_map/ppermute | solution.py:43
  123.6 14.3 %collective-permute-start.13 = (bf16[4,192,192]{1,2,0:T(8,128)(2,1)S(1)}, bf16[4,192,192]{1,2,0:T(8,128)(2,1)S(1)}, u32[]{:S(2)}, u32[]{:S(2)}) collective-permute-start(bf16[4,192,192]{1,2,0:T(8,128)(2,1)S(1)} %get-tuple-element.26), channel_id=1, source_target_pairs={{0,7},{1,0},{2,1},{3,2},{4,3},{5,4},{6,5},{7,6},{8,15},{9,8},{10,9... | collective-permute-start | bytes 884744 | tf_op jit(solution)/shard_map/ppermute | solution.py:43
  131.8 12.5 %collective-permute-start.10 = (bf16[4,192,192]{1,2,0:T(8,128)(2,1)S(1)}, bf16[4,192,192]{1,2,0:T(8,128)(2,1)S(1)}, u32[]{:S(2)}, u32[]{:S(2)}) collective-permute-start(bf16[4,192,192]{1,2,0:T(8,128)(2,1)S(1)} %fusion.18), channel_id=1, source_target_pairs={{0,1},{1,2},{2,3},{3,4},{4,5},{5,6},{6,7},{7,0},{8,9},{9,10},{10,1... | collective-permute-start | bytes 884744 | tf_op jit(solution)/shard_map/ppermute | solution.py:43
  145.8 11.6 %collective-permute-start.11 = (bf16[4,192,192]{1,2,0:T(8,128)(2,1)S(1)}, bf16[4,192,192]{1,2,0:T(8,128)(2,1)S(1)}, u32[]{:S(2)}, u32[]{:S(2)}) collective-permute-start(bf16[4,192,192]{1,2,0:T(8,128)(2,1)S(1)} %get-tuple-element.24), channel_id=1, source_target_pairs={{0,1},{1,2},{2,3},{3,4},{4,5},{5,6},{6,7},{7,0},{8,9},{9,10},{10,1... | collective-permute-start | bytes 884744 | tf_op jit(solution)/shard_map/ppermute | solution.py:43
  147.7 10.5 %collective-permute-start.14 = (bf16[4,192,192]{1,2,0:T(8,128)(2,1)S(1)}, bf16[4,192,192]{1,2,0:T(8,128)(2,1)S(1)}, u32[]{:S(2)}, u32[]{:S(2)}) collective-permute-start(bf16[4,192,192]{1,2,0:T(8,128)(2,1)S(1)} %get-tuple-element.25), channel_id=1, source_target_pairs={{0,7},{1,0},{2,1},{3,2},{4,3},{5,4},{6,5},{7,6},{8,15},{9,8},{10,9... | collective-permute-start | bytes 884744 | tf_op jit(solution)/shard_map/ppermute | solution.py:43
  159.8 10.6 %collective-permute-start.12 = (bf16[4,192,192]{1,2,0:T(8,128)(2,1)S(1)}, bf16[4,192,192]{1,2,0:T(8,128)(2,1)S(1)}, u32[]{:S(2)}, u32[]{:S(2)}) collective-permute-start(bf16[4,192,192]{1,2,0:T(8,128)(2,1)S(1)} %get-tuple-element.22), channel_id=1, source_target_pairs={{0,1},{1,2},{2,3},{3,4},{4,5},{5,6},{6,7},{7,0},{8,9},{9,10},{10,1... | collective-permute-start | bytes 884744 | tf_op jit(solution)/shard_map/ppermute | solution.py:43
  165.1 10.1 %collective-permute-start.15 = (bf16[4,192,192]{1,2,0:T(8,128)(2,1)S(1)}, bf16[4,192,192]{1,2,0:T(8,128)(2,1)S(1)}, u32[]{:S(2)}, u32[]{:S(2)}) collective-permute-start(bf16[4,192,192]{1,2,0:T(8,128)(2,1)S(1)} %get-tuple-element.23), channel_id=1, source_target_pairs={{0,7},{1,0},{2,1},{3,2},{4,3},{5,4},{6,5},{7,6},{8,15},{9,8},{10,9... | collective-permute-start | bytes 884744 | tf_op jit(solution)/shard_map/ppermute | solution.py:43
  176.5 7.5 %collective-permute-start.16 = (bf16[192,192]{0,1:T(8,128)(2,1)S(1)}, bf16[192,192]{0,1:T(8,128)(2,1)S(1)}, u32[]{:S(2)}, u32[]{:S(2)}) collective-permute-start(bf16[192,192]{0,1:T(8,128)(2,1)S(1)} %get-tuple-element.30), channel_id=1, source_target_pairs={{0,8},{8,16},{16,24},{24,0},{1,9},{9,17},{17,25},{25,1},{2,10},{10... | collective-permute-start | bytes 221192 | tf_op jit(solution)/shard_map/ppermute | solution.py:43
  179.3 7.2 %collective-permute-start.18 = (bf16[192,192]{0,1:T(8,128)(2,1)S(1)}, bf16[192,192]{0,1:T(8,128)(2,1)S(1)}, u32[]{:S(2)}, u32[]{:S(2)}) collective-permute-start(bf16[192,192]{0,1:T(8,128)(2,1)S(1)} %get-tuple-element.31), channel_id=1, source_target_pairs={{0,24},{8,0},{16,8},{24,16},{1,25},{9,1},{17,9},{25,17},{2,26},{10... | collective-permute-start | bytes 221192 | tf_op jit(solution)/shard_map/ppermute | solution.py:43
  184.0 7.9 %collective-permute-start.17 = (bf16[192,192]{0,1:T(8,128)(2,1)S(1)}, bf16[192,192]{0,1:T(8,128)(2,1)S(1)}, u32[]{:S(2)}, u32[]{:S(2)}) collective-permute-start(bf16[192,192]{0,1:T(8,128)(2,1)S(1)} %fusion.29), channel_id=1, source_target_pairs={{0,8},{8,16},{16,24},{24,0},{1,9},{9,17},{17,25},{25,1},{2,10},{10... | collective-permute-start | bytes 221192 | tf_op jit(solution)/shard_map/ppermute | solution.py:43
where the time goes:
time: 224 us; the launch traced here: 223 us
  starting transfers between devices  71.7 us (32%)
  blocking collectives  55.8 us (25%)
  waiting for transfers between devices  41.5 us (19%)
  local copies, waits for them, and re-layouts  23.1 us (10%)
  matrix products  19.5 us (9%)
  other arithmetic  9.77 us (4%)
    ppermute x17, starting transfers between devices, shift(): return lax.ppermute(x, self.axis, perm=pairs)  56.1 us
    ppermute x17, waiting for transfers between devices, shift(): return lax.ppermute(x, self.axis, perm=pairs)  38.6 us
    all_gather x1, blocking collectives, shards(): by_dp = lax.all_gather(over_seq, 'dp', axis=0, tiled=False)  18.7 us
    ppermute x2, starting transfers between devices, dp_partner(): return lax.ppermute(x, 'dp', perm=pairs)  15.6 us
    all_gather x1, blocking collectives, shards(): stack_y = lax.all_gather(w_mine, 'fh', axis=0, tiled=False)  13.7 us
    all_gather x1, blocking collectives, shards(): packed_all = lax.all_gather(packed, 'seq', axis=0, tiled=True)  12.4 us
    all_gather x1, blocking collectives, shards(): by_seq = lax.all_gather(over_fsdp, 'seq', axis=0, tiled=False)  11 us
    unnamed x23, local copies, waits for them, and re-layouts  9.48 us
  transfers between devices with their start and end apart: 19, of which 16 were waited for; matrix products, arithmetic and copies ran while one was open for 11% of the time, Pallas kernels for 0%

commit v1 on v0

--- a/solution.py
+++ b/solution.py
@@ -3,6 +3,12 @@
 import jax.numpy as jnp
 from jax import lax
 from jax.sharding import PartitionSpec as P
+
+
+def laid_out(blocks, dim):
+    dims = list(blocks.shape[1:])
+    dims[dim] *= blocks.shape[0]
+    return jnp.moveaxis(blocks, 0, dim).reshape(dims)
 
 
 def contract_first(left, right):
@@ -141,7 +147,19 @@
     me_x = ring_x.position()
     ids_col = jnp.broadcast_to(image_ids.astype(jnp.bfloat16)[:, None], (n_rows, width_head))
     packed = jnp.concatenate([heads, grad_out, ids_col], axis=1)
-    packed_all = lax.all_gather(packed, "seq", axis=0, tiled=True)
+    size_2 = lax.axis_size("seq")
+    pairs_2 = [(i_2, (i_2 + 1) % size_2) for i_2 in range(size_2)]
+    back = [(b, a_2) for a_2, b in pairs_2]
+    lower, upper = ([], [])
+    for step_2 in range(size_2 - 1):
+        if step_2 % 2 == 0:
+            lower.append(lax.ppermute(lower[-1] if lower else packed, "seq", pairs_2))
+        else:
+            upper.append(lax.ppermute(upper[-1] if upper else packed, "seq", back))
+    blocks_2 = jnp.stack([*lower[::-1], packed, *upper])
+    shift_2 = lax.axis_index("seq") - len(lower)
+    blocks_2 = blocks_2[(jnp.arange(size_2) - shift_2) % size_2]
+    packed_all = laid_out(blocks_2, 0)
     query_all = packed_all[:, :width_head]
     keys_all = packed_all[:, width_head : 2 * width_head]
     values_all = packed_all[:, 2 * width_head : 3 * width_head]

time: 224 us -> 248 us (1.11)
  the two profiles are of different devices: /device:TPU:75 before, /device:TPU:1 now
where the time goes in v1:
time: 248 us; the launch traced here: 247 us
  starting transfers between devices  81.6 us (33%)
  waiting for transfers between devices  51.1 us (21%)
  blocking collectives  43.3 us (17%)
  local copies, waits for them, and re-layouts  29.1 us (12%)
  matrix products  26.6 us (11%)
  other arithmetic  13.8 us (6%)
    ppermute x17, starting transfers between devices, shift(): return lax.ppermute(x, self.axis, perm=pairs)  58.5 us
    ppermute x17, waiting for transfers between devices, shift(): return lax.ppermute(x, self.axis, perm=pairs)  36.4 us
    all_gather x1, blocking collectives, shards(): by_dp = lax.all_gather(over_seq, 'dp', axis=0, tiled=False)  16.3 us
    all_gather x1, blocking collectives, shards(): stack_y = lax.all_gather(w_mine, 'fh', axis=0, tiled=False)  16.3 us
    ppermute x2, starting transfers between devices, dp_partner(): return lax.ppermute(x, 'dp', perm=pairs)  14.7 us
    ppermute x2, waiting for transfers between devices, shards(): lower.append(lax.ppermute(lower[-1] if lower else packed, 'seq', pairs_2))  11.7 us
    unnamed x27, local copies, waits for them, and re-layouts  11.7 us
    all_gather x1, blocking collectives, shards(): by_seq = lax.all_gather(over_fsdp, 'seq', axis=0, tiled=False)  10.7 us
  transfers between devices with their start and end apart: 22, of which 18 were waited for; matrix products, arithmetic and copies ran while one was open for 10% of the time, Pallas kernels for 0%

profile of v1, /device:TPU:1, one launch (start us, length us, event | category | flops | bytes accessed | tf_op | source)
XLA Modules:
  0.0 246.8 jit_solution(13203423899966054638)
XLA Ops:
  1.6 16.3 %all-gather = bf16[768,192]{1,0:T(8,128)(2,1)S(1)} all-gather(bf16[192,192]{1,0:T(8,128)(2,1)S(1)} %constant_dynamic-slice_fusion), channel_id=2, replica_groups=mesh['dp'=4,'seq'=4,'fh'=4,'fz'=8] {'fh'}, dimensions={0}, use_global_device_ids=true | all-gather | bytes 368640 | tf_op jit(solution)/shard_map/all_gather | solution.py:127
  17.9 3.2 %collective-permute-start = (bf16[4,192,192]{2,1,0:T(8,128)(2,1)S(1)}, bf16[4,192,192]{2,1,0:T(8,128)(2,1)}, u32[]{:S(2)}, u32[]{:S(2)}) collective-permute-start(bf16[4,192,192]{2,1,0:T(8,128)(2,1)S(1)} %bitcast.124), channel_id=1, source_target_pairs={{0,1},{1,2},{2,3},{3,4},{4,5},{5,6},{6,7},{7,0},{8,9},{9,10},{10,1... | collective-permute-start | bytes 884744 | tf_op jit(solution)/shard_map/ppermute | solution.py:49
  21.2 8.6 %collective-permute-start.1 = (bf16[4,192,192]{2,1,0:T(8,128)(2,1)S(1)}, bf16[4,192,192]{2,1,0:T(8,128)(2,1)S(1)}, u32[]{:S(2)}, u32[]{:S(2)}) collective-permute-start(bf16[4,192,192]{2,1,0:T(8,128)(2,1)S(1)} %bitcast.125), channel_id=1, source_target_pairs={{0,7},{1,0},{2,1},{3,2},{4,3},{5,4},{6,5},{7,6},{8,15},{9,8},{10,9... | collective-permute-start | bytes 884744 | tf_op jit(solution)/shard_map/ppermute | solution.py:49
  36.8 4.6 %collective-permute-start.3 = (bf16[4,192,192]{2,1,0:T(8,128)(2,1)S(1)}, bf16[4,192,192]{2,1,0:T(8,128)(2,1)S(1)}, u32[]{:S(2)}, u32[]{:S(2)}) collective-permute-start(bf16[4,192,192]{2,1,0:T(8,128)(2,1)S(1)} %collective-permute-done.1), channel_id=1, source_target_pairs={{0,7},{1,0},{2,1},{3,2},{4,3},{5,4},{6,5},{7,6},{8,15},{9,8},{10,9... | collective-permute-start | bytes 884744 | tf_op jit(solution)/shard_map/ppermute | solution.py:49
  46.0 5.0 %collective-permute-start.5 = (bf16[4,192,192]{2,1,0:T(8,128)(2,1)S(1)}, bf16[4,192,192]{2,1,0:T(8,128)(2,1)S(1)}, u32[]{:S(2)}, u32[]{:S(2)}) collective-permute-start(bf16[4,192,192]{2,1,0:T(8,128)(2,1)S(1)} %collective-permute-done.3), channel_id=1, source_target_pairs={{0,7},{1,0},{2,1},{3,2},{4,3},{5,4},{6,5},{7,6},{8,15},{9,8},{10,9... | collective-permute-start | bytes 884744 | tf_op jit(solution)/shard_map/ppermute | solution.py:49
  56.8 4.5 %reshape.193 = bf16[192,4,8,192]{3,2,1,0:T(8,128)(2,1)} reshape(bf16[192,6144]{1,0:T(8,128)(2,1)S(1)} %bitcast.113) | data formatting | bytes 4718592 | tf_op jit(solution)/shard_map/reshape | solution.py:128
  65.8 2.6 %gather_fusion.1 = bf16[32,192,192]{2,1,0:T(8,128)(2,1)S(1)} fusion(bf16[32,192,192]{2,1,0:T(8,128)(2,1)} %bitcast.114, s32[1024]{0:T(1024)S(1)} %pad_clamp_fusion.1), kind=kCustom, calls=%fused_computation.1 | custom fusion | bytes 4718720 | tf_op jit(solution)/shard_map/jit(_take)/gather | solution.py:135
  68.5 2.6 %copy.33 = bf16[6144,192]{0,1:T(8,128)(2,1)} copy(bf16[6144,192]{1,0:T(8,128)(2,1)S(1)} %bitcast.110) | data formatting | bytes 4718592 | tf_op jit(solution)/shard_map/reshape | solution.py:135
  71.1 10.5 %collective-permute-start.7 = (bf16[6144,192]{0,1:T(8,128)(2,1)}, bf16[6144,192]{0,1:T(8,128)(2,1)}, u32[]{:S(2)}, u32[]{:S(2)}) collective-permute-start(bf16[6144,192]{0,1:T(8,128)(2,1)} %copy.33), channel_id=1, source_target_pairs={{0,128},{128,0},{256,384},{384,256},{1,129},{129,1},{257,385},{385... | collective-permute-start | bytes 7077896 | tf_op jit(solution)/shard_map/ppermute | solution.py:28
  81.6 2.6 %convolution_bitcast_fusion.1 = bf16[192,192]{1,0:T(8,128)(2,1)S(1)} fusion(bf16[6144,192]{1,0:T(8,128)(2,1)S(1)} %bitcast.111, bf16[1,192,6144]{2,1,0:T(8,128)(2,1)} %param.5), kind=kOutput, calls=%fused_computation.22 | convolution fusion | flops 452984832 | bytes 4792320 | tf_op jit(solution)/shard_map/dot_general | solution.py:137
  89.5 3.1 %collective-permute-start.8 = (bf16[192,640]{1,0:T(8,128)(2,1)}, bf16[192,640]{1,0:T(8,128)(2,1)}, u32[]{:S(2)}, u32[]{:S(2)}) collective-permute-start(bf16[192,640]{1,0:T(8,128)(2,1)} %get-tuple-element.33), channel_id=1, source_target_pairs={{0,32},{32,64},{64,96},{96,0},{1,33},{33,65},{65,97},{97,1},{2,34}... | collective-permute-start | bytes 737288 | tf_op jit(solution)/shard_map/ppermute | solution.py:156
  92.6 3.4 %collective-permute-start.10 = (bf16[192,640]{1,0:T(8,128)(2,1)}, bf16[192,640]{1,0:T(8,128)(2,1)}, u32[]{:S(2)}, u32[]{:S(2)}) collective-permute-start(bf16[192,640]{1,0:T(8,128)(2,1)} %get-tuple-element.33), channel_id=1, source_target_pairs={{32,0},{64,32},{96,64},{0,96},{33,1},{65,33},{97,65},{1,97},{34,2}... | collective-permute-start | bytes 737288 | tf_op jit(solution)/shard_map/ppermute | solution.py:158
  96.0 4.1 %collective-permute-done.8 = bf16[192,640]{1,0:T(8,128)(2,1)} collective-permute-done((bf16[192,640]{1,0:T(8,128)(2,1)}, bf16[192,640]{1,0:T(8,128)(2,1)}, u32[]{:S(2)}, u32[]{:S(2)}) %collective-permute-start.8) | collective-permute-done | bytes 245792 | tf_op jit(solution)/shard_map/ppermute | solution.py:156
  102.0 7.7 %collective-permute-done.9 = bf16[192,640]{1,0:T(8,128)(2,1)} collective-permute-done((bf16[192,640]{1,0:T(8,128)(2,1)}, bf16[192,640]{1,0:T(8,128)(2,1)}, u32[]{:S(2)}, u32[]{:S(2)}) %collective-permute-start.9) | collective-permute-done | bytes 245792 | tf_op jit(solution)/shard_map/ppermute | solution.py:156
  112.0 2.8 %gather_fusion.2 = bf16[4,192,640]{2,1,0:T(8,128)(2,1)} fusion(bf16[4,192,640]{2,1,0:T(8,128)(2,1)} %pad_maximum_fusion, s32[1024]{0:T(1024)S(1)} %pad_clamp_fusion), kind=kCustom, calls=%fused_computation.2 | custom fusion | bytes 1966096 | tf_op jit(solution)/shard_map/gather | solution.py:161
  125.1 2.9 %multiply_convert_fusion = bf16[768,768]{0,1:T(8,128)(2,1)S(1)} fusion(f32[768,768]{0,1:T(8,128)} %copy-done.6, f32[768]{0:T(1024)S(1)} %fusion.13, f32[768]{0:T(1024)S(1)} %log_add_fusion, bf16[768]{0:T(1024)(128)(2,1)S(1)} %slice_reduce_fusion, bf16[768,640]{1,0:T(8,128)(2,1)} %bitcast.120), kind=kOutput, calls=%fused_computation.17 | convolution fusion | flops 155713536 | bytes 3944448 | tf_op jit(solution)/shard_map/dot_general | solution.py:21
  130.5 4.1 %convert_bitcast_fusion = bf16[8,4,192,192]{2,3,0,1:T(8,128)(2,1)} fusion(bf16[192,4,8,192]{3,2,1,0:T(8,128)(2,1)S(1)} %copy-done.1, pred[]{:T(512)S(6)} %eq.41, bf16[192,128]{1,0:T(8,128)(2,1)S(1)} %convolution_convert_fusion.1, bf16[192,128]{1,0:T(8,128)(2,1)S(1)} %convolution_convert_fusion.2, bf16[192,128]{1,0:T(8,128)(2,1)S(1)} %convolution_convert_fusion), kind=kOutput, calls=%fused_computation.9 | convolution fusion | flops 454496256 | bytes 4866049 | tf_op jit(solution)/shard_map/pyzd,pc->zydc/dot_general | solution.py:194
  134.7 4.2 %collective-permute-start.11 = (bf16[8,4,192,192]{2,3,0,1:T(8,128)(2,1)}, bf16[8,4,192,192]{2,3,0,1:T(8,128)(2,1)}, u32[]{:S(2)}, u32[]{:S(2)}) collective-permute-start(bf16[8,4,192,192]{2,3,0,1:T(8,128)(2,1)} %convert_bitcast_fusion), channel_id=1, source_target_pairs={{0,128},{128,0},{256,384},{384,256},{1,129},{129,1},{257,385},{385... | collective-permute-start | bytes 7077896 | tf_op jit(solution)/shard_map/ppermute | solution.py:28
  144.3 3.0 %convert_add_fusion = f32[8,4,192,192]{2,3,0,1:T(8,128)S(1)} fusion(f32[8,4,192,192]{2,3,0,1:T(8,128)S(1)} %fusion.5, bf16[8,4,192,192]{2,3,0,1:T(8,128)(2,1)} %collective-permute-done.11), kind=kLoop, calls=%fused_computation.5 | loop fusion | flops 2359296 | bytes 11796480 | tf_op jit(solution)/shard_map/add | solution.py:198
  149.4 4.0 %fusion = bf16[192,6144]{1,0:T(8,128)(2,1)} fusion(f32[192,6144]{1,0:T(8,128)S(1)} %fusion.54, bf16[6144,192]{0,1:T(8,128)(2,1)} %collective-permute-done.7, pred[]{:T(512)S(6)} %eq.41, bf16[192,128]{1,0:T(8,128)(2,1)S(1)} %convolution_convert_fusion.1, bf16[192,128]{1,0:T(8,128)(2,1)S(1)} %convolution_convert_fusion.2, ...), kind=kOutput, calls=%fused_computation.4 | convolution fusion | flops 455675904 | bytes 9584641 | tf_op jit(solution)/shard_map/dot_general | solution.py:21
  153.3 4.5 %collective-permute-start.16 = (bf16[4,192,192]{1,2,0:T(8,128)(2,1)S(1)}, bf16[4,192,192]{1,2,0:T(8,128)(2,1)S(1)}, u32[]{:S(2)}, u32[]{:S(2)}) collective-permute-start(bf16[4,192,192]{1,2,0:T(8,128)(2,1)S(1)} %get-tuple-element.26), channel_id=1, source_target_pairs={{0,7},{1,0},{2,1},{3,2},{4,3},{5,4},{6,5},{7,6},{8,15},{9,8},{10,9... | collective-permute-start | bytes 884744 | tf_op jit(solution)/shard_map/ppermute | solution.py:49
  157.9 3.0 %collective-permute-done.12 = bf16[4,192,192]{1,2,0:T(8,128)(2,1)S(1)} collective-permute-done((bf16[4,192,192]{1,2,0:T(8,128)(2,1)S(1)}, bf16[4,192,192]{1,2,0:T(8,128)(2,1)S(1)}, u32[]{:S(2)}, u32[]{:S(2)}) %collective-permute-start.12) | collective-permute-done | bytes 294944 | tf_op jit(solution)/shard_map/ppermute | solution.py:49
  163.0 2.7 %collective-permute-done.16 = bf16[4,192,192]{1,2,0:T(8,128)(2,1)S(1)} collective-permute-done((bf16[4,192,192]{1,2,0:T(8,128)(2,1)S(1)}, bf16[4,192,192]{1,2,0:T(8,128)(2,1)S(1)}, u32[]{:S(2)}, u32[]{:S(2)}) %collective-permute-start.16) | collective-permute-done | bytes 294944 | tf_op jit(solution)/shard_map/ppermute | solution.py:49
  165.6 7.9 %collective-permute-done.13 = bf16[4,192,192]{1,2,0:T(8,128)(2,1)S(1)} collective-permute-done((bf16[4,192,192]{1,2,0:T(8,128)(2,1)S(1)}, bf16[4,192,192]{1,2,0:T(8,128)(2,1)S(1)}, u32[]{:S(2)}, u32[]{:S(2)}) %collective-permute-start.13) | collective-permute-done | bytes 294944 | tf_op jit(solution)/shard_map/ppermute | solution.py:49
  177.0 4.6 %collective-permute-start.17 = (bf16[4,192,192]{1,2,0:T(8,128)(2,1)S(1)}, bf16[4,192,192]{1,2,0:T(8,128)(2,1)S(1)}, u32[]{:S(2)}, u32[]{:S(2)}) collective-permute-start(bf16[4,192,192]{1,2,0:T(8,128)(2,1)S(1)} %get-tuple-element.25), channel_id=1, source_target_pairs={{0,7},{1,0},{2,1},{3,2},{4,3},{5,4},{6,5},{7,6},{8,15},{9,8},{10,9... | collective-permute-start | bytes 884744 | tf_op jit(solution)/shard_map/ppermute | solution.py:49
  181.6 5.0 %collective-permute-done.14 = bf16[4,192,192]{1,2,0:T(8,128)(2,1)S(1)} collective-permute-done((bf16[4,192,192]{1,2,0:T(8,128)(2,1)S(1)}, bf16[4,192,192]{1,2,0:T(8,128)(2,1)S(1)}, u32[]{:S(2)}, u32[]{:S(2)}) %collective-permute-start.14) | collective-permute-done | bytes 294944 | tf_op jit(solution)/shard_map/ppermute | solution.py:49
  191.0 5.3 %collective-permute-start.18 = (bf16[4,192,192]{1,2,0:T(8,128)(2,1)S(1)}, bf16[4,192,192]{1,2,0:T(8,128)(2,1)S(1)}, u32[]{:S(2)}, u32[]{:S(2)}) collective-permute-start(bf16[4,192,192]{1,2,0:T(8,128)(2,1)S(1)} %get-tuple-element.23), channel_id=1, source_target_pairs={{0,7},{1,0},{2,1},{3,2},{4,3},{5,4},{6,5},{7,6},{8,15},{9,8},{10,9... | collective-permute-start | bytes 884744 | tf_op jit(solution)/shard_map/ppermute | solution.py:49
  196.4 4.1 %collective-permute-done.15 = bf16[4,192,192]{1,2,0:T(8,128)(2,1)S(1)} collective-permute-done((bf16[4,192,192]{1,2,0:T(8,128)(2,1)S(1)}, bf16[4,192,192]{1,2,0:T(8,128)(2,1)S(1)}, u32[]{:S(2)}, u32[]{:S(2)}) %collective-permute-start.15) | collective-permute-done | bytes 294944 | tf_op jit(solution)/shard_map/ppermute | solution.py:49
  205.0 5.5 %collective-permute-start.21 = (bf16[192,192]{0,1:T(8,128)(2,1)S(1)}, bf16[192,192]{0,1:T(8,128)(2,1)S(1)}, u32[]{:S(2)}, u32[]{:S(2)}) collective-permute-start(bf16[192,192]{0,1:T(8,128)(2,1)S(1)} %get-tuple-element.31), channel_id=1, source_target_pairs={{0,24},{8,0},{16,8},{24,16},{1,25},{9,1},{17,9},{25,17},{2,26},{10... | collective-permute-start | bytes 221192 | tf_op jit(solution)/shard_map/ppermute | solution.py:49
  213.2 5.5 %collective-permute-done.20 = bf16[192,192]{0,1:T(8,128)(2,1)S(1)} collective-permute-done((bf16[192,192]{0,1:T(8,128)(2,1)S(1)}, bf16[192,192]{0,1:T(8,128)(2,1)S(1)}, u32[]{:S(2)}, u32[]{:S(2)}) %collective-permute-start.20) | collective-permute-done | bytes 73760 | tf_op jit(solution)/shard_map/ppermute | solution.py:49
  218.9 10.7 %all-gather.1 = f32[768,192]{1,0:T(8,128)S(1)} all-gather(f32[192,192]{1,0:T(8,128)S(1)} %copy.42), channel_id=3, replica_groups=mesh['dp'=4,'seq'=4,'fh'=4,'fz'=8] {'seq'}, dimensions={0}, use_global_device_ids=true | all-gather | bytes 737280 | tf_op jit(solution)/shard_map/all_gather | solution.py:201
  229.6 16.3 %all_gather.20 = f32[4,192,192]{2,1,0:T(8,128)S(1)} all-gather(f32[1,192,192]{2,1,0:T(8,128)S(1)} %fusion.28), channel_id=1, replica_groups=mesh['dp'=4,'seq'=4,'fh'=4,'fz'=8] {'dp'}, dimensions={0}, use_global_device_ids=true | all-gather | bytes 737280 | tf_op jit(solution)/shard_map/all_gather | solution.py:205
  (89 shorter events, 70.6 us)
Async XLA Ops:
  0.6 0.9 copy-start
  17.9 15.2 %collective-permute-start = (bf16[4,192,192]{2,1,0:T(8,128)(2,1)S(1)}, bf16[4,192,192]{2,1,0:T(8,128)(2,1)}, u32[]{:S(2)}, u32[]{:S(2)}) collective-permute-start(bf16[4,192,192]{2,1,0:T(8,128)(2,1)S(1)} %bitcast.124), channel_id=1, source_target_pairs={{0,1},{1,2},{2,3},{3,4},{4,5},{5,6},{6,7},{7,0},{8,9},{9,10},{10,1... | collective-permute-start | bytes 884744 | tf_op jit(solution)/shard_map/ppermute | solution.py:49
  21.2 15.6 %collective-permute-start.1 = (bf16[4,192,192]{2,1,0:T(8,128)(2,1)S(1)}, bf16[4,192,192]{2,1,0:T(8,128)(2,1)S(1)}, u32[]{:S(2)}, u32[]{:S(2)}) collective-permute-start(bf16[4,192,192]{2,1,0:T(8,128)(2,1)S(1)} %bitcast.125), channel_id=1, source_target_pairs={{0,7},{1,0},{2,1},{3,2},{4,3},{5,4},{6,5},{7,6},{8,15},{9,8},{10,9... | collective-permute-start | bytes 884744 | tf_op jit(solution)/shard_map/ppermute | solution.py:49
  30.5 26.2 %copy-start.4 = (bf16[1,192,6144]{2,1,0:T(8,128)(2,1)S(1)}, bf16[1,192,6144]{2,1,0:T(8,128)(2,1)}, u32[]{:S(2)}) copy-start(bf16[1,192,6144]{2,1,0:T(8,128)(2,1)} %param.5) | copy-start | bytes 7077892
  33.1 9.9 %collective-permute-start.2 = (bf16[4,192,192]{2,1,0:T(8,128)(2,1)}, bf16[4,192,192]{2,1,0:T(8,128)(2,1)S(1)}, u32[]{:S(2)}, u32[]{:S(2)}) collective-permute-start(bf16[4,192,192]{2,1,0:T(8,128)(2,1)} %collective-permute-done), channel_id=1, source_target_pairs={{0,1},{1,2},{2,3},{3,4},{4,5},{5,6},{6,7},{7,0},{8,9},{9,10},{10,1... | collective-permute-start | bytes 884744 | tf_op jit(solution)/shard_map/ppermute | solution.py:49
  36.8 9.3 %collective-permute-start.3 = (bf16[4,192,192]{2,1,0:T(8,128)(2,1)S(1)}, bf16[4,192,192]{2,1,0:T(8,128)(2,1)S(1)}, u32[]{:S(2)}, u32[]{:S(2)}) collective-permute-start(bf16[4,192,192]{2,1,0:T(8,128)(2,1)S(1)} %collective-permute-done.1), channel_id=1, source_target_pairs={{0,7},{1,0},{2,1},{3,2},{4,3},{5,4},{6,5},{7,6},{8,15},{9,8},{10,9... | collective-permute-start | bytes 884744 | tf_op jit(solution)/shard_map/ppermute | solution.py:49
  43.0 10.0 %collective-permute-start.4 = (bf16[4,192,192]{2,1,0:T(8,128)(2,1)S(1)}, bf16[4,192,192]{2,1,0:T(8,128)(2,1)}, u32[]{:S(2)}, u32[]{:S(2)}) collective-permute-start(bf16[4,192,192]{2,1,0:T(8,128)(2,1)S(1)} %collective-permute-done.2), channel_id=1, source_target_pairs={{0,1},{1,2},{2,3},{3,4},{4,5},{5,6},{6,7},{7,0},{8,9},{9,10},{10,1... | collective-permute-start | bytes 884744 | tf_op jit(solution)/shard_map/ppermute | solution.py:49
  46.0 10.7 %collective-permute-start.5 = (bf16[4,192,192]{2,1,0:T(8,128)(2,1)S(1)}, bf16[4,192,192]{2,1,0:T(8,128)(2,1)S(1)}, u32[]{:S(2)}, u32[]{:S(2)}) collective-permute-start(bf16[4,192,192]{2,1,0:T(8,128)(2,1)S(1)} %collective-permute-done.3), channel_id=1, source_target_pairs={{0,7},{1,0},{2,1},{3,2},{4,3},{5,4},{6,5},{7,6},{8,15},{9,8},{10,9... | collective-permute-start | bytes 884744 | tf_op jit(solution)/shard_map/ppermute | solution.py:49
  53.0 11.0 %collective-permute-start.6 = (bf16[4,192,192]{2,1,0:T(8,128)(2,1)}, bf16[4,192,192]{2,1,0:T(8,128)(2,1)}, u32[]{:S(2)}, u32[]{:S(2)}) collective-permute-start(bf16[4,192,192]{2,1,0:T(8,128)(2,1)} %collective-permute-done.4), channel_id=1, source_target_pairs={{0,1},{1,2},{2,3},{3,4},{4,5},{5,6},{6,7},{7,0},{8,9},{9,10},{10,1... | collective-permute-start | bytes 884744 | tf_op jit(solution)/shard_map/ppermute | solution.py:49
  68.5 13.1 %copy-start.8 = (s32[1,192]{1,0:T(1,128)S(1)}, s32[1,192]{1,0:T(1,128)}, u32[]{:S(2)}) copy-start(s32[1,192]{1,0:T(1,128)} %param.6) | copy-start | bytes 2308
  71.1 14.9 %collective-permute-start.7 = (bf16[6144,192]{0,1:T(8,128)(2,1)}, bf16[6144,192]{0,1:T(8,128)(2,1)}, u32[]{:S(2)}, u32[]{:S(2)}) collective-permute-start(bf16[6144,192]{0,1:T(8,128)(2,1)} %copy.33), channel_id=1, source_target_pairs={{0,128},{128,0},{256,384},{384,256},{1,129},{129,1},{257,385},{385... | collective-permute-start | bytes 7077896 | tf_op jit(solution)/shard_map/ppermute | solution.py:28
  81.6 4.4 %copy-start.5 = (bf16[1,192,6144]{2,1,0:T(8,128)(2,1)S(1)}, bf16[1,192,6144]{2,1,0:T(8,128)(2,1)}, u32[]{:S(2)}) copy-start(bf16[1,192,6144]{2,1,0:T(8,128)(2,1)} %param.5) | copy-start | bytes 7077892
  84.2 4.5 %copy-start.7 = (bf16[1,192,128]{2,1,0:T(8,128)(2,1)S(1)}, bf16[1,192,128]{2,1,0:T(8,128)(2,1)}, u32[]{:S(2)}) copy-start(bf16[1,192,128]{2,1,0:T(8,128)(2,1)} %param.8) | copy-start | bytes 147460
  89.5 10.6 %collective-permute-start.8 = (bf16[192,640]{1,0:T(8,128)(2,1)}, bf16[192,640]{1,0:T(8,128)(2,1)}, u32[]{:S(2)}, u32[]{:S(2)}) collective-permute-start(bf16[192,640]{1,0:T(8,128)(2,1)} %get-tuple-element.33), channel_id=1, source_target_pairs={{0,32},{32,64},{64,96},{96,0},{1,33},{33,65},{65,97},{97,1},{2,34}... | collective-permute-start | bytes 737288 | tf_op jit(solution)/shard_map/ppermute | solution.py:156
  92.6 9.4 %collective-permute-start.10 = (bf16[192,640]{1,0:T(8,128)(2,1)}, bf16[192,640]{1,0:T(8,128)(2,1)}, u32[]{:S(2)}, u32[]{:S(2)}) collective-permute-start(bf16[192,640]{1,0:T(8,128)(2,1)} %get-tuple-element.33), channel_id=1, source_target_pairs={{32,0},{64,32},{96,64},{0,96},{33,1},{65,33},{97,65},{1,97},{34,2}... | collective-permute-start | bytes 737288 | tf_op jit(solution)/shard_map/ppermute | solution.py:158
  100.0 9.7 %collective-permute-start.9 = (bf16[192,640]{1,0:T(8,128)(2,1)}, bf16[192,640]{1,0:T(8,128)(2,1)}, u32[]{:S(2)}, u32[]{:S(2)}) collective-permute-start(bf16[192,640]{1,0:T(8,128)(2,1)} %collective-permute-done.8), channel_id=1, source_target_pairs={{0,32},{32,64},{64,96},{96,0},{1,33},{33,65},{65,97},{97,1},{2,34}... | collective-permute-start | bytes 737288 | tf_op jit(solution)/shard_map/ppermute | solution.py:156
  118.3 1.4 copy-start.6
  125.1 5.4 %copy-start.1 = (bf16[192,4,8,192]{3,2,1,0:T(8,128)(2,1)S(1)}, bf16[192,4,8,192]{3,2,1,0:T(8,128)(2,1)}, u32[]{:S(2)}) copy-start(bf16[192,4,8,192]{3,2,1,0:T(8,128)(2,1)} %reshape.193) | copy-start | bytes 7077892
  134.7 9.7 %collective-permute-start.11 = (bf16[8,4,192,192]{2,3,0,1:T(8,128)(2,1)}, bf16[8,4,192,192]{2,3,0,1:T(8,128)(2,1)}, u32[]{:S(2)}, u32[]{:S(2)}) collective-permute-start(bf16[8,4,192,192]{2,3,0,1:T(8,128)(2,1)} %convert_bitcast_fusion), channel_id=1, source_target_pairs={{0,128},{128,0},{256,384},{384,256},{1,129},{129,1},{257,385},{385... | collective-permute-start | bytes 7077896 | tf_op jit(solution)/shard_map/ppermute | solution.py:28
  138.9 1.9 copy-start.2
  147.3 13.5 %copy-start.3 = (f32[8,4,192,192]{2,3,0,1:T(8,128)}, f32[8,4,192,192]{2,3,0,1:T(8,128)S(1)}, u32[]{:S(2)}) copy-start(f32[8,4,192,192]{2,3,0,1:T(8,128)S(1)} %convert_add_fusion) | copy-start | bytes 14155780
  147.5 13.4 %collective-permute-start.12 = (bf16[4,192,192]{1,2,0:T(8,128)(2,1)S(1)}, bf16[4,192,192]{1,2,0:T(8,128)(2,1)S(1)}, u32[]{:S(2)}, u32[]{:S(2)}) collective-permute-start(bf16[4,192,192]{1,2,0:T(8,128)(2,1)S(1)} %get-tuple-element.27), channel_id=1, source_target_pairs={{0,1},{1,2},{2,3},{3,4},{4,5},{5,6},{6,7},{7,0},{8,9},{9,10},{10,1... | collective-permute-start | bytes 884744 | tf_op jit(solution)/shard_map/ppermute | solution.py:49
  153.3 12.3 %collective-permute-start.16 = (bf16[4,192,192]{1,2,0:T(8,128)(2,1)S(1)}, bf16[4,192,192]{1,2,0:T(8,128)(2,1)S(1)}, u32[]{:S(2)}, u32[]{:S(2)}) collective-permute-start(bf16[4,192,192]{1,2,0:T(8,128)(2,1)S(1)} %get-tuple-element.26), channel_id=1, source_target_pairs={{0,7},{1,0},{2,1},{3,2},{4,3},{5,4},{6,5},{7,6},{8,15},{9,8},{10,9... | collective-permute-start | bytes 884744 | tf_op jit(solution)/shard_map/ppermute | solution.py:49
  161.0 12.5 %collective-permute-start.13 = (bf16[4,192,192]{1,2,0:T(8,128)(2,1)S(1)}, bf16[4,192,192]{1,2,0:T(8,128)(2,1)S(1)}, u32[]{:S(2)}, u32[]{:S(2)}) collective-permute-start(bf16[4,192,192]{1,2,0:T(8,128)(2,1)S(1)} %fusion.18), channel_id=1, source_target_pairs={{0,1},{1,2},{2,3},{3,4},{4,5},{5,6},{6,7},{7,0},{8,9},{9,10},{10,1... | collective-permute-start | bytes 884744 | tf_op jit(solution)/shard_map/ppermute | solution.py:49
  175.1 11.6 %collective-permute-start.14 = (bf16[4,192,192]{1,2,0:T(8,128)(2,1)S(1)}, bf16[4,192,192]{1,2,0:T(8,128)(2,1)S(1)}, u32[]{:S(2)}, u32[]{:S(2)}) collective-permute-start(bf16[4,192,192]{1,2,0:T(8,128)(2,1)S(1)} %get-tuple-element.24), channel_id=1, source_target_pairs={{0,1},{1,2},{2,3},{3,4},{4,5},{5,6},{6,7},{7,0},{8,9},{9,10},{10,1... | collective-permute-start | bytes 884744 | tf_op jit(solution)/shard_map/ppermute | solution.py:49
  177.0 10.6 %collective-permute-start.17 = (bf16[4,192,192]{1,2,0:T(8,128)(2,1)S(1)}, bf16[4,192,192]{1,2,0:T(8,128)(2,1)S(1)}, u32[]{:S(2)}, u32[]{:S(2)}) collective-permute-start(bf16[4,192,192]{1,2,0:T(8,128)(2,1)S(1)} %get-tuple-element.25), channel_id=1, source_target_pairs={{0,7},{1,0},{2,1},{3,2},{4,3},{5,4},{6,5},{7,6},{8,15},{9,8},{10,9... | collective-permute-start | bytes 884744 | tf_op jit(solution)/shard_map/ppermute | solution.py:49
  189.1 11.4 %collective-permute-start.15 = (bf16[4,192,192]{1,2,0:T(8,128)(2,1)S(1)}, bf16[4,192,192]{1,2,0:T(8,128)(2,1)S(1)}, u32[]{:S(2)}, u32[]{:S(2)}) collective-permute-start(bf16[4,192,192]{1,2,0:T(8,128)(2,1)S(1)} %get-tuple-element.22), channel_id=1, source_target_pairs={{0,1},{1,2},{2,3},{3,4},{4,5},{5,6},{6,7},{7,0},{8,9},{9,10},{10,1... | collective-permute-start | bytes 884744 | tf_op jit(solution)/shard_map/ppermute | solution.py:49
  191.0 10.7 %collective-permute-start.18 = (bf16[4,192,192]{1,2,0:T(8,128)(2,1)S(1)}, bf16[4,192,192]{1,2,0:T(8,128)(2,1)S(1)}, u32[]{:S(2)}, u32[]{:S(2)}) collective-permute-start(bf16[4,192,192]{1,2,0:T(8,128)(2,1)S(1)} %get-tuple-element.23), channel_id=1, source_target_pairs={{0,7},{1,0},{2,1},{3,2},{4,3},{5,4},{6,5},{7,6},{8,15},{9,8},{10,9... | collective-permute-start | bytes 884744 | tf_op jit(solution)/shard_map/ppermute | solution.py:49
  203.0 8.2 %collective-permute-start.19 = (bf16[192,192]{0,1:T(8,128)(2,1)S(1)}, bf16[192,192]{0,1:T(8,128)(2,1)S(1)}, u32[]{:S(2)}, u32[]{:S(2)}) collective-permute-start(bf16[192,192]{0,1:T(8,128)(2,1)S(1)} %get-tuple-element.30), channel_id=1, source_target_pairs={{0,8},{8,16},{16,24},{24,0},{1,9},{9,17},{17,25},{25,1},{2,10},{10... | collective-permute-start | bytes 221192 | tf_op jit(solution)/shard_map/ppermute | solution.py:49
  205.0 8.2 %collective-permute-start.21 = (bf16[192,192]{0,1:T(8,128)(2,1)S(1)}, bf16[192,192]{0,1:T(8,128)(2,1)S(1)}, u32[]{:S(2)}, u32[]{:S(2)}) collective-permute-start(bf16[192,192]{0,1:T(8,128)(2,1)S(1)} %get-tuple-element.31), channel_id=1, source_target_pairs={{0,24},{8,0},{16,8},{24,16},{1,25},{9,1},{17,9},{25,17},{2,26},{10... | collective-permute-start | bytes 221192 | tf_op jit(solution)/shard_map/ppermute | solution.py:49
  211.2 7.5 %collective-permute-start.20 = (bf16[192,192]{0,1:T(8,128)(2,1)S(1)}, bf16[192,192]{0,1:T(8,128)(2,1)S(1)}, u32[]{:S(2)}, u32[]{:S(2)}) collective-permute-start(bf16[192,192]{0,1:T(8,128)(2,1)S(1)} %fusion.29), channel_id=1, source_target_pairs={{0,8},{8,16},{16,24},{24,0},{1,9},{9,17},{17,25},{25,1},{2,10},{10... | collective-permute-start | bytes 221192 | tf_op jit(solution)/shard_map/ppermute | solution.py:49
